TPU v7x, 32 devices: a whole 2x2x4 slice. The times are simulated.
32 devices in a mesh: tract: 2 (over x), skyx: 4 (over y, core), skyy: 4 (over z).
Axes of the slice: x: 2, y: 2, z: 4, core: 2. Of those that a mesh axis runs over, the one named last changes fastest.
Arguments:
- images: bfloat16 [8, 8, 136, 4480], P(('tract', 'skyy'), 'skyx'), parts along dimension 0, may hold values from -6 to 6
- masks: int32 [8, 8, 136, 4480], P(('tract', 'skyy'), 'skyx'), parts along dimension 0, may hold values 0 or 1
- row_kernels: bfloat16 [8, 8, 128, 136], P(('tract', 'skyy'), 'skyx'), parts along dimension 0, may hold values from -1 to 2
- col_kernel: bfloat16 [66, 384, 128], P('tract'), parts along dimension 0, may hold values from -1 to 2
- inv_var: float32 [8, 8], P(('tract', 'skyy')), parts along dimension 0, may hold values from 0.5 to 4
- dest_col: int32 [8, 128, 1], P(('tract', 'skyy'), 'skyx'), parts along dimension 0, may hold values from 0 to 3; in each aligned block of 32 rows (0 to 31, 32 to 63, ..., all dimensions but the last counted through in order) at most 12 rows name the same one
- dest_row: int32 [8, 128], P(('tract', 'skyy'), 'skyx'), parts along dimension 0, may hold values from 0 to 31
Outputs:
- coadd: float32 [1024, 15872], P(('tract', 'skyy'), 'skyx'), parts along dimension 0
There are 2 independent parts, one for each index of `tract`. A program takes and returns all parts, laid end to end along the dimension named above; each array names one. Nothing has to cross between parts.
Inputs may be any that keep to these rules, and one draw needn't show every extreme that they name: `dest_col`: the 32 row blocks of any one device name one patch column at most 12 times, and some device names one exactly 12 times.
All inputs are finite; a program needn't handle non-finite values. No bound on the sum of `masks` on one device may be relied on, other than what follows from the above.
Results may differ from a plain program's by a relative error of at most 0.0057.
Values may be sent and summed in bfloat16 or wider, within the bound.
No kernel may reach another device: no remote copies, remote signals or barrier semaphores. Data moves between devices by JAX's collectives and lax.ppermute only.
A program may use at most 128 MiB of HBM per device.

v0:
```python
import jax
import jax.numpy as jnp
from jax import lax
from jax.experimental import pallas as pl
from jax.experimental.pallas import tpu as pltpu
from jax.sharding import PartitionSpec as P


OVY = 64
PR = 128
RB = 8
SPLIT = (5, 8, 6, 3, 2, 9)
ORDER = (0, 5, 1, 2, 3, 4)
ROW_PIECE = 640


def shifted(value, axis, steps):
    count = lax.axis_size(axis)
    first, last = (max(0, -steps), min(count, count - steps))
    return lax.ppermute(value, axis, [(source, source + steps) for source in range(first, last)])


def make_warp_kernel(start, width, first_tile, exposures, groups):
    def kernel(w_ref, idx_ref, img_hbm, mask_hbm, rk_ref, ck_hbm, prev_ref, *refs):
        out_refs = refs[:groups]
        img_buf, mask_buf, rw_buf, blk_buf, ck_ref, sems = refs[groups:]
        ph = rk_ref.shape[2]
        tiles, kw, tw = ck_ref.shape
        blocks = ph // RB
        ck_copy = pltpu.make_async_copy(ck_hbm.at[pl.ds(first_tile, tiles)], ck_ref, sems.at[2, 0])
        ck_copy.start()
        copies = []
        for e in range(exposures):
            ci = pltpu.make_async_copy(img_hbm.at[0, e, :, pl.ds(start, width)], img_buf.at[e], sems.at[0, e])
            cm = pltpu.make_async_copy(mask_hbm.at[0, e, :, pl.ds(start, width)], mask_buf.at[e], sems.at[1, e])
            ci.start()
            cm.start()
            copies.append((ci, cm))
        for e in range(exposures):
            ci, cm = copies[e]
            ci.wait()
            cm.wait()
            rk = rk_ref[0, e]
            if e == 0:
                ck_copy.wait()
            piece_start = 0
            while piece_start < width:
                piece = min(ROW_PIECE, width - piece_start)
                cols = pl.ds(piece_start, piece)
                good = mask_buf[e, :, cols] == 0
                img = img_buf[e, :, cols]
                p0 = jnp.where(good, img, jnp.zeros_like(img))
                p1 = good.astype(jnp.bfloat16)
                rw_buf[0:ph, cols] = jnp.dot(rk, p0, preferred_element_type=jnp.float32).astype(jnp.bfloat16)
                rw_buf[ph : 2 * ph, cols] = jnp.dot(rk, p1, preferred_element_type=jnp.float32).astype(jnp.bfloat16)
                piece_start += piece
            weight = w_ref[e]

            def tile(t, carry):
                off = pl.multiple_of(t * tw, tw)
                x = rw_buf[:, pl.ds(off, kw)]
                r = jnp.dot(x, ck_ref[t], preferred_element_type=jnp.float32) * weight
                rows = pl.ds(e * blocks, blocks)
                blk_buf[rows, 0, :, pl.ds(off, tw)] = r[0:ph].reshape(blocks, RB, tw).astype(jnp.bfloat16)
                blk_buf[rows, 1, :, pl.ds(off, tw)] = r[ph : 2 * ph].reshape(blocks, RB, tw).astype(jnp.bfloat16)
                return carry

            lax.fori_loop(0, tiles, tile, 0)

        capacity = out_refs[0].shape[0]
        for g in range(groups):
            def gather(slot, carry, g=g):
                out_refs[g][slot] = blk_buf[idx_ref[g * capacity + slot]]
                return carry

            lax.fori_loop(0, capacity, gather, 0)

    return kernel


def warp_chunk(first_tile, per, groups, weights, send_idx, images, masks, row_kernels, col_kernel, previous):
    _, exposures, hin, _ = images.shape
    ph = row_kernels.shape[2]
    _, kw, tw = col_kernel.shape
    width = per * tw
    window = width + kw - tw
    start = first_tile * tw
    blocks = ph // RB
    slots = send_idx.shape[0]
    return pl.pallas_call(
        make_warp_kernel(start, window, first_tile, exposures, groups),
        in_specs=[
            pl.BlockSpec(memory_space=pltpu.SMEM),
            pl.BlockSpec(memory_space=pltpu.SMEM),
            pl.BlockSpec(memory_space=pl.ANY),
            pl.BlockSpec(memory_space=pl.ANY),
            pl.BlockSpec(memory_space=pltpu.VMEM),
            pl.BlockSpec(memory_space=pl.ANY),
            pl.BlockSpec(memory_space=pl.ANY),
        ],
        out_specs=[pl.BlockSpec(memory_space=pltpu.VMEM)] * groups,
        out_shape=[jax.ShapeDtypeStruct((slots // groups, 2, RB, width), jnp.bfloat16)] * groups,
        scratch_shapes=[
            pltpu.VMEM((exposures, hin, window), jnp.bfloat16),
            pltpu.VMEM((exposures, hin, window), jnp.int32),
            pltpu.VMEM((2 * ph, window), jnp.bfloat16),
            pltpu.VMEM((exposures * blocks, 2, RB, width), jnp.bfloat16),
            pltpu.VMEM((per, kw, tw), jnp.bfloat16),
            pltpu.SemaphoreType.DMA((3, exposures)),
        ],
        compiler_params=pltpu.CompilerParams(vmem_limit_bytes=48 * 1024 * 1024),
        cost_estimate=pl.CostEstimate(
            flops=exposures * (8 * ph * hin * window + 4 * ph * kw * width),
            transcendentals=0,
            bytes_accessed=exposures * hin * window * 6 + per * kw * tw * 2 + slots * 2 * RB * width * 2,
        ),
    )(weights, send_idx, images, masks, row_kernels, col_kernel, previous)


def make_place_kernel(groups, capacity, positions, margin, inner):
    def kernel(rows_ref, *refs):
        recv_refs = refs[:groups]
        upper_ref, lower_ref, int_ref, canvas = refs[-4:]
        canvas[...] = jnp.zeros(canvas.shape, jnp.float32)
        for g in range(groups):
            def body(c, carry, g=g):
                pos = rows_ref[g * capacity + c]

                @pl.when((pos >= 0) & (pos < positions))
                def _():
                    canvas[pos] += recv_refs[g][c].astype(jnp.float32)

                return carry

            lax.fori_loop(0, capacity, body, 0)
        upper_ref[...] = canvas[0:margin].astype(jnp.bfloat16)
        lower_ref[...] = canvas[margin + inner :].astype(jnp.bfloat16)
        int_ref[...] = canvas[margin : margin + inner]

    return kernel


def place(rows, recvs, after, positions, margin, inner):
    after = list(after)
    groups = len(recvs)
    capacity = recvs[0].shape[0]
    block = recvs[0].shape[1:]
    return pl.pallas_call(
        make_place_kernel(groups, capacity, positions, margin, inner),
        in_specs=[pl.BlockSpec(memory_space=pltpu.SMEM)]
        + [pl.BlockSpec(memory_space=pltpu.VMEM)] * groups
        + [pl.BlockSpec(memory_space=pl.ANY)] * len(after),
        out_specs=[pl.BlockSpec(memory_space=pltpu.VMEM)] * 3,
        out_shape=[
            jax.ShapeDtypeStruct((margin,) + block, jnp.bfloat16),
            jax.ShapeDtypeStruct((margin,) + block, jnp.bfloat16),
            jax.ShapeDtypeStruct((inner,) + block, jnp.float32),
        ],
        scratch_shapes=[pltpu.VMEM((positions,) + block, jnp.float32)],
        compiler_params=pltpu.CompilerParams(vmem_limit_bytes=32 * 1024 * 1024),
    )(rows, *recvs, *after)


def local_body(images, masks, row_kernels, col_kernel, inv_var, dest_col, dest_row):
    exposures = images.shape[1]
    tile_width = col_kernel.shape[2]
    cw = col_kernel.shape[0] * tile_width
    pw = cw - 2 * tile_width
    tiles = col_kernel.shape[0]
    bounds = [tiles * sum(SPLIT[:i]) // sum(SPLIT) for i in range(len(SPLIT) + 1)]
    first_exp = lax.axis_index("skyx") * exposures
    weights = lax.dynamic_slice_in_dim(inv_var[0], first_exp, exposures)

    slot_dest = dest_col[0, :, 0]
    slot_rows = dest_row[0]
    slot_count = slot_dest.shape[0]
    peers = lax.axis_size("skyx")
    capacity = max(2, (3 * slot_count + 2 * peers - 1) // (2 * peers))
    positions = (PR + 2 * OVY) // RB
    offsets = (slot_dest - lax.axis_index("skyx")) % peers
    earlier = (jnp.arange(slot_count)[None, :] < jnp.arange(slot_count)[:, None]).astype(jnp.int32)
    onehot_dest = (offsets[:, None] == jnp.arange(peers)[None, :]).astype(jnp.int32)
    ranks = jnp.sum(jnp.dot(earlier, onehot_dest) * onehot_dest, axis=1)
    chosen = (offsets[None, None, :] == jnp.arange(peers)[:, None, None]) & (
        ranks[None, None, :] == jnp.arange(capacity)[None, :, None]
    )
    send_rows = jnp.sum(jnp.where(chosen, slot_rows[None, None, :] + 1, 0), axis=2) - 1
    send_idx = jnp.sum(jnp.where(chosen, jnp.arange(slot_count)[None, None, :] + 1, 0), axis=2) - 1
    send_idx = jnp.clip(send_idx, 0, slot_count - 1).reshape(-1)
    rings = [[(i, (i + step) % peers) for i in range(peers)] for step in range(peers)]
    recv_rows = [send_rows[0]] + [lax.ppermute(send_rows[step], "skyx", rings[step]) for step in range(1, peers)]
    recv_rows = jnp.concatenate(recv_rows)
    recv_rows = recv_rows.reshape(-1)

    margin = OVY // RB
    inner = PR // RB
    interiors = {}
    after = [recv_rows]
    previous = send_idx
    for chunk in ORDER:
        per = bounds[chunk + 1] - bounds[chunk]
        send_buf = warp_chunk(bounds[chunk], per, peers, weights, send_idx, images, masks, row_kernels, col_kernel, previous)
        previous = send_buf[-1]
        recvs = [send_buf[0]] + [lax.ppermute(send_buf[step], "skyx", rings[step]) for step in range(1, peers)]
        upper, lower, interior = place(recv_rows, recvs, after, positions, margin, inner)
        from_above = shifted(lower, "skyy", 1)
        from_below = shifted(upper, "skyy", -1)
        from_above = from_above.astype(jnp.float32)
        from_below = from_below.astype(jnp.float32)
        after = [upper]
        interior = interior.at[:margin].add(from_above)
        interior = interior.at[inner - margin :].add(from_below)
        interiors[chunk] = interior

    left_edge = interiors[0]
    right_edge = interiors[len(SPLIT) - 1]
    width = right_edge.shape[-1]
    from_left = shifted(right_edge[..., width - tile_width :].astype(jnp.bfloat16), "skyx", 1)
    from_right = shifted(left_edge[..., :tile_width].astype(jnp.bfloat16), "skyx", -1)
    from_left = from_left.astype(jnp.float32)
    from_right = from_right.astype(jnp.float32)
    first = left_edge[..., tile_width:]
    first = first.at[..., :tile_width].add(from_left)
    last = right_edge[..., : width - tile_width]
    last = last.at[..., width - 2 * tile_width :].add(from_right)
    middle = [interiors[c] for c in range(1, len(SPLIT) - 1)]
    core = jnp.concatenate([first] + middle + [last], axis=-1)
    num = core[:, 0].reshape(PR, pw)
    den = core[:, 1].reshape(PR, pw)
    return num / jnp.maximum(den, 1.0)


def solution(mesh):
    in_specs = (
        P(("tract", "skyy"), "skyx", None, None),
        P(("tract", "skyy"), "skyx", None, None),
        P(("tract", "skyy"), "skyx", None, None),
        P("tract", None, None),
        P(("tract", "skyy"), None),
        P(("tract", "skyy"), "skyx", None),
        P(("tract", "skyy"), "skyx"),
    )
    out_specs = P(("tract", "skyy"), "skyx")
    return jax.shard_map(local_body, mesh=mesh, in_specs=in_specs, out_specs=out_specs, check_vma=False)
```

profile of v0, /device:TPU:1, one launch (start us, length us, event | category | flops | bytes accessed | tf_op | source)
XLA Modules:
  0.0 181.4 jit_solution(17772316512026457042)
XLA Ops:
  5.0 4.8 %shard_map.73 = (bf16[12,2,8,640]{3,2,1,0:T(8,128)(2,1)S(1)}, bf16[12,2,8,640]{3,2,1,0:T(8,128)(2,1)S(1)}, bf16[12,2,8,640]{3,2,1,0:T(8,128)(2,1)S(1)}, bf16[12,2,8,640]{3,2,1,0:T(8,128)(2,1)S(1)}) custom-call(f32[2]{0:T(128)S(1)} %fusion.15.w_ref, s32[48]{0:T(128)S(1)} %min.12.idx_ref.prev_ref, bf16[1,2,136,4480]{3,2,1,0:T(8,128)(2,1)S(1)} %copy-done.1, ...), custom_call_target="tpu_custom_call" | custom-call | flops 501219328 | bytes 2936832 | tf_op jit(solution)/shard_map/pallas_call | solution.py:90
  9.8 2.7 %collective-permute-start.3 = (bf16[12,2,8,640]{3,2,1,0:T(8,128)(2,1)S(1)}, bf16[12,2,8,640]{3,2,1,0:T(8,128)(2,1)S(1)}, u32[]{:S(2)}, u32[]{:S(2)}) collective-permute-start(bf16[12,2,8,640]{3,2,1,0:T(8,128)(2,1)S(1)} %get-tuple-element.216), channel_id=1, source_target_pairs={{0,4},{4,8},{8,12},{12,0},{1,5},{5,9},{9,13},{13,1},{2,6},{6,10},{... | collective-permute-start | bytes 737288 | tf_op jit(solution)/shard_map/ppermute | solution.py:204
  12.5 6.9 %shard_map.75 = (bf16[12,2,8,1152]{3,2,1,0:T(8,128)(2,1)S(1)}, bf16[12,2,8,1152]{3,2,1,0:T(8,128)(2,1)S(1)}, bf16[12,2,8,1152]{3,2,1,0:T(8,128)(2,1)S(1)}, bf16[12,2,8,1152]{3,2,1,0:T(8,128)(2,1)S(1)}) custom-call(f32[2]{0:T(128)S(1)} %fusion.15.w_ref, s32[48]{0:T(128)S(1)} %min.12.idx_ref.prev_ref, bf16[1,2,136,4480]{3,2,1,0:T(8,128)(2,1)S(1)} %copy-done.1, ...), custom_call_target="tpu_custom_call" | custom-call | flops 845152256 | bytes 4952064 | tf_op jit(solution)/shard_map/pallas_call | solution.py:90
  19.4 6.3 %shard_map.77 = (bf16[12,2,8,1024]{3,2,1,0:T(8,128)(2,1)S(1)}, bf16[12,2,8,1024]{3,2,1,0:T(8,128)(2,1)S(1)}, bf16[12,2,8,1024]{3,2,1,0:T(8,128)(2,1)S(1)}, bf16[12,2,8,1024]{3,2,1,0:T(8,128)(2,1)S(1)}) custom-call(f32[2]{0:T(128)S(1)} %fusion.15.w_ref, s32[48]{0:T(128)S(1)} %min.12.idx_ref.prev_ref, bf16[1,2,136,4480]{3,2,1,0:T(8,128)(2,1)S(1)} %copy-done.1, ...), custom_call_target="tpu_custom_call" | custom-call | flops 759169024 | bytes 4448256 | tf_op jit(solution)/shard_map/pallas_call | solution.py:90
  25.7 5.3 %shard_map.79 = (bf16[12,2,8,768]{3,2,1,0:T(8,128)(2,1)S(1)}, bf16[12,2,8,768]{3,2,1,0:T(8,128)(2,1)S(1)}, bf16[12,2,8,768]{3,2,1,0:T(8,128)(2,1)S(1)}, bf16[12,2,8,768]{3,2,1,0:T(8,128)(2,1)S(1)}) custom-call(f32[2]{0:T(128)S(1)} %fusion.15.w_ref, s32[48]{0:T(128)S(1)} %min.12.idx_ref.prev_ref, bf16[1,2,136,4480]{3,2,1,0:T(8,128)(2,1)S(1)} %copy-done.1, ...), custom_call_target="tpu_custom_call" | custom-call | flops 587202560 | bytes 3440640 | tf_op jit(solution)/shard_map/pallas_call | solution.py:90
  31.0 3.8 %shard_map.81 = (bf16[12,2,8,384]{3,2,1,0:T(8,128)(2,1)S(1)}, bf16[12,2,8,384]{3,2,1,0:T(8,128)(2,1)S(1)}, bf16[12,2,8,384]{3,2,1,0:T(8,128)(2,1)S(1)}, bf16[12,2,8,384]{3,2,1,0:T(8,128)(2,1)S(1)}) custom-call(f32[2]{0:T(128)S(1)} %fusion.15.w_ref, s32[48]{0:T(128)S(1)} %min.12.idx_ref.prev_ref, bf16[1,2,136,4480]{3,2,1,0:T(8,128)(2,1)S(1)} %copy-done.1, ...), custom_call_target="tpu_custom_call" | custom-call | flops 329252864 | bytes 1929216 | tf_op jit(solution)/shard_map/pallas_call | solution.py:90
  37.3 4.4 %collective-permute-done.2 = s32[12]{0:T(128)S(1)} collective-permute-done((s32[12]{0:T(128)S(1)}, s32[12]{0:T(128)S(1)}, u32[]{:S(2)}, u32[]{:S(2)}) %collective-permute-start.2) | collective-permute-done | bytes 80 | tf_op jit(solution)/shard_map/ppermute | solution.py:191
  49.5 4.7 %collective-permute-done.5.refs_3_ = bf16[12,2,8,640]{3,2,1,0:T(8,128)(2,1)S(1)} collective-permute-done((bf16[12,2,8,640]{3,2,1,0:T(8,128)(2,1)S(1)}, bf16[12,2,8,640]{3,2,1,0:T(8,128)(2,1)S(1)}, u32[]{:S(2)}, u32[]{:S(2)}) %collective-permute-start.5) | collective-permute-done | bytes 245792 | tf_op jit(solution)/shard_map/ppermute | solution.py:204
  55.1 8.0 %collective-permute-done.19.refs_1_ = bf16[12,2,8,768]{3,2,1,0:T(8,128)(2,1)S(1)} collective-permute-done((bf16[12,2,8,768]{3,2,1,0:T(8,128)(2,1)S(1)}, bf16[12,2,8,768]{3,2,1,0:T(8,128)(2,1)S(1)}, u32[]{:S(2)}, u32[]{:S(2)}) %collective-permute-start.19) | collective-permute-done | bytes 294944 | tf_op jit(solution)/shard_map/ppermute | solution.py:204
  65.6 5.4 %collective-permute-done.20.refs_2_ = bf16[12,2,8,768]{3,2,1,0:T(8,128)(2,1)S(1)} collective-permute-done((bf16[12,2,8,768]{3,2,1,0:T(8,128)(2,1)S(1)}, bf16[12,2,8,768]{3,2,1,0:T(8,128)(2,1)S(1)}, u32[]{:S(2)}, u32[]{:S(2)}) %collective-permute-start.20) | collective-permute-done | bytes 294944 | tf_op jit(solution)/shard_map/ppermute | solution.py:204
  74.4 5.0 %collective-permute-done.15.refs_2_ = bf16[12,2,8,1024]{3,2,1,0:T(8,128)(2,1)S(1)} collective-permute-done((bf16[12,2,8,1024]{3,2,1,0:T(8,128)(2,1)S(1)}, bf16[12,2,8,1024]{3,2,1,0:T(8,128)(2,1)S(1)}, u32[]{:S(2)}, u32[]{:S(2)}) %collective-permute-start.15) | collective-permute-done | bytes 393248 | tf_op jit(solution)/shard_map/ppermute | solution.py:204
  79.4 3.5 %collective-permute-start.6 = (bf16[8,2,8,640]{3,2,1,0:T(8,128)(2,1)S(1)}, bf16[8,2,8,640]{3,2,1,0:T(8,128)(2,1)S(1)}, u32[]{:S(2)}, u32[]{:S(2)}) collective-permute-start(bf16[8,2,8,640]{3,2,1,0:T(8,128)(2,1)S(1)} %get-tuple-element.220), channel_id=1, source_target_pairs={{0,1},{1,2},{2,3},{4,5},{5,6},{6,7},{8,9},{9,10},{10,11},{12,13},{... | collective-permute-start | bytes 491528 | tf_op jit(solution)/shard_map/ppermute | solution.py:20
  82.9 3.3 %shard_map.83 = (bf16[12,2,8,256]{3,2,1,0:T(8,128)(2,1)S(1)}, bf16[12,2,8,256]{3,2,1,0:T(8,128)(2,1)S(1)}, bf16[12,2,8,256]{3,2,1,0:T(8,128)(2,1)S(1)}, bf16[12,2,8,256]{3,2,1,0:T(8,128)(2,1)S(1)}) custom-call(f32[2]{0:T(128)S(1)} %fusion.15.w_ref, s32[48]{0:T(128)S(1)} %min.12.idx_ref.prev_ref, bf16[1,2,136,4480]{3,2,1,0:T(8,128)(2,1)S(1)} %copy-done.1, ...), custom_call_target="tpu_custom_call" | custom-call | flops 243269632 | bytes 1425408 | tf_op jit(solution)/shard_map/pallas_call | solution.py:90
  86.2 14.0 %collective-permute-done.16.refs_3_ = bf16[12,2,8,1024]{3,2,1,0:T(8,128)(2,1)S(1)} collective-permute-done((bf16[12,2,8,1024]{3,2,1,0:T(8,128)(2,1)S(1)}, bf16[12,2,8,1024]{3,2,1,0:T(8,128)(2,1)S(1)}, u32[]{:S(2)}, u32[]{:S(2)}) %collective-permute-start.16) | collective-permute-done | bytes 393248 | tf_op jit(solution)/shard_map/ppermute | solution.py:204
  111.6 4.2 %collective-permute-start.32 = (bf16[8,2,8,256]{3,2,1,0:T(8,128)(2,1)S(1)}, bf16[8,2,8,256]{3,2,1,0:T(8,128)(2,1)S(1)}, u32[]{:S(2)}, u32[]{:S(2)}) collective-permute-start(bf16[8,2,8,256]{3,2,1,0:T(8,128)(2,1)S(1)} %get-tuple-element.255), channel_id=1, source_target_pairs={{0,1},{1,2},{2,3},{4,5},{5,6},{6,7},{8,9},{9,10},{10,11},{12,13},{... | collective-permute-start | bytes 196616 | tf_op jit(solution)/shard_map/ppermute | solution.py:20
  116.0 3.8 %collective-permute-start.34 = (bf16[16,2,8,128]{3,2,1,0:T(8,128)(2,1)S(1)}, bf16[16,2,8,128]{3,2,1,0:T(8,128)(2,1)S(1)}, u32[]{:S(2)}, u32[]{:S(2)}) collective-permute-start(bf16[16,2,8,128]{3,2,1,0:T(8,128)(2,1)S(1)} %slice.524), channel_id=1, source_target_pairs={{4,0},{8,4},{12,8},{5,1},{9,5},{13,9},{6,2},{10,6},{14,10},{7,3},{... | collective-permute-start | bytes 196616 | tf_op jit(solution)/shard_map/ppermute | solution.py:20
  125.1 16.6 %collective-permute-done.33 = bf16[8,2,8,256]{3,2,1,0:T(8,128)(2,1)S(1)} collective-permute-done((bf16[8,2,8,256]{3,2,1,0:T(8,128)(2,1)S(1)}, bf16[8,2,8,256]{3,2,1,0:T(8,128)(2,1)S(1)}, u32[]{:S(2)}, u32[]{:S(2)}) %collective-permute-start.33) | collective-permute-done | bytes 65568 | tf_op jit(solution)/shard_map/ppermute | solution.py:20
  141.7 3.4 %collective-permute-start.27 = (bf16[8,2,8,384]{3,2,1,0:T(8,128)(2,1)S(1)}, bf16[8,2,8,384]{3,2,1,0:T(8,128)(2,1)S(1)}, u32[]{:S(2)}, u32[]{:S(2)}) collective-permute-start(bf16[8,2,8,384]{3,2,1,0:T(8,128)(2,1)S(1)} %get-tuple-element.248), channel_id=1, source_target_pairs={{0,1},{1,2},{2,3},{4,5},{5,6},{6,7},{8,9},{9,10},{10,11},{12,13},{... | collective-permute-start | bytes 294920 | tf_op jit(solution)/shard_map/ppermute | solution.py:20
  148.0 4.9 %collective-permute-done.28 = bf16[8,2,8,384]{3,2,1,0:T(8,128)(2,1)S(1)} collective-permute-done((bf16[8,2,8,384]{3,2,1,0:T(8,128)(2,1)S(1)}, bf16[8,2,8,384]{3,2,1,0:T(8,128)(2,1)S(1)}, u32[]{:S(2)}, u32[]{:S(2)}) %collective-permute-start.28) | collective-permute-done | bytes 98336 | tf_op jit(solution)/shard_map/ppermute | solution.py:20
  152.9 3.4 %collective-permute-start.22 = (bf16[8,2,8,768]{3,2,1,0:T(8,128)(2,1)S(1)}, bf16[8,2,8,768]{3,2,1,0:T(8,128)(2,1)S(1)}, u32[]{:S(2)}, u32[]{:S(2)}) collective-permute-start(bf16[8,2,8,768]{3,2,1,0:T(8,128)(2,1)S(1)} %get-tuple-element.241), channel_id=1, source_target_pairs={{0,1},{1,2},{2,3},{4,5},{5,6},{6,7},{8,9},{9,10},{10,11},{12,13},{... | collective-permute-start | bytes 589832 | tf_op jit(solution)/shard_map/ppermute | solution.py:20
  158.9 3.8 %collective-permute-start.17 = (bf16[8,2,8,1024]{3,2,1,0:T(8,128)(2,1)S(1)}, bf16[8,2,8,1024]{3,2,1,0:T(8,128)(2,1)S(1)}, u32[]{:S(2)}, u32[]{:S(2)}) collective-permute-start(bf16[8,2,8,1024]{3,2,1,0:T(8,128)(2,1)S(1)} %get-tuple-element.234), channel_id=1, source_target_pairs={{0,1},{1,2},{2,3},{4,5},{5,6},{6,7},{8,9},{9,10},{10,11},{12,13},{... | collective-permute-start | bytes 786440 | tf_op jit(solution)/shard_map/ppermute | solution.py:20
  162.8 3.2 %collective-permute-start.11 = (bf16[8,2,8,1152]{3,2,1,0:T(8,128)(2,1)S(1)}, bf16[8,2,8,1152]{3,2,1,0:T(8,128)(2,1)S(1)}, u32[]{:S(2)}, u32[]{:S(2)}) collective-permute-start(bf16[8,2,8,1152]{3,2,1,0:T(8,128)(2,1)S(1)} %get-tuple-element.227), channel_id=1, source_target_pairs={{0,1},{1,2},{2,3},{4,5},{5,6},{6,7},{8,9},{9,10},{10,11},{12,13},{... | collective-permute-start | bytes 884744 | tf_op jit(solution)/shard_map/ppermute | solution.py:20
  166.4 5.7 %collective-permute-done.11 = bf16[8,2,8,1152]{3,2,1,0:T(8,128)(2,1)S(1)} collective-permute-done((bf16[8,2,8,1152]{3,2,1,0:T(8,128)(2,1)S(1)}, bf16[8,2,8,1152]{3,2,1,0:T(8,128)(2,1)S(1)}, u32[]{:S(2)}, u32[]{:S(2)}) %collective-permute-start.11) | collective-permute-done | bytes 294944 | tf_op jit(solution)/shard_map/ppermute | solution.py:20
  172.5 5.7 %collective-permute-start.13 = (bf16[16,2,8,128]{3,2,1,0:T(8,128)(2,1)S(1)}, bf16[16,2,8,128]{3,2,1,0:T(8,128)(2,1)S(1)}, u32[]{:S(2)}, u32[]{:S(2)}) collective-permute-start(bf16[16,2,8,128]{3,2,1,0:T(8,128)(2,1)S(1)} %slice.525), channel_id=1, source_target_pairs={{0,4},{4,8},{8,12},{1,5},{5,9},{9,13},{2,6},{6,10},{10,14},{3,7},{... | collective-permute-start | bytes 196616 | tf_op jit(solution)/shard_map/ppermute | solution.py:20
  (101 shorter events, 48.2 us)
Async XLA Ops:
  9.8 38.6 %collective-permute-start.3 = (bf16[12,2,8,640]{3,2,1,0:T(8,128)(2,1)S(1)}, bf16[12,2,8,640]{3,2,1,0:T(8,128)(2,1)S(1)}, u32[]{:S(2)}, u32[]{:S(2)}) collective-permute-start(bf16[12,2,8,640]{3,2,1,0:T(8,128)(2,1)S(1)} %get-tuple-element.216), channel_id=1, source_target_pairs={{0,4},{4,8},{8,12},{12,0},{1,5},{5,9},{9,13},{13,1},{2,6},{6,10},{... | collective-permute-start | bytes 737288 | tf_op jit(solution)/shard_map/ppermute | solution.py:204
  12.5 36.7 %collective-permute-start.4 = (bf16[12,2,8,640]{3,2,1,0:T(8,128)(2,1)S(1)}, bf16[12,2,8,640]{3,2,1,0:T(8,128)(2,1)S(1)}, u32[]{:S(2)}, u32[]{:S(2)}) collective-permute-start(bf16[12,2,8,640]{3,2,1,0:T(8,128)(2,1)S(1)} %get-tuple-element.217), channel_id=1, source_target_pairs={{0,8},{4,12},{8,0},{12,4},{1,9},{5,13},{9,1},{13,5},{2,10},{6,14},... | collective-permute-start | bytes 737288 | tf_op jit(solution)/shard_map/ppermute | solution.py:204
  34.8 12.5 %collective-permute-start.24 = (bf16[12,2,8,384]{3,2,1,0:T(8,128)(2,1)S(1)}, bf16[12,2,8,384]{3,2,1,0:T(8,128)(2,1)S(1)}, u32[]{:S(2)}, u32[]{:S(2)}) collective-permute-start(bf16[12,2,8,384]{3,2,1,0:T(8,128)(2,1)S(1)} %get-tuple-element.244), channel_id=1, source_target_pairs={{0,4},{4,8},{8,12},{12,0},{1,5},{5,9},{9,13},{13,1},{2,6},{6,10},{... | collective-permute-start | bytes 442376 | tf_op jit(solution)/shard_map/ppermute | solution.py:204
  34.9 13.0 %collective-permute-start.25 = (bf16[12,2,8,384]{3,2,1,0:T(8,128)(2,1)S(1)}, bf16[12,2,8,384]{3,2,1,0:T(8,128)(2,1)S(1)}, u32[]{:S(2)}, u32[]{:S(2)}) collective-permute-start(bf16[12,2,8,384]{3,2,1,0:T(8,128)(2,1)S(1)} %get-tuple-element.245), channel_id=1, source_target_pairs={{0,8},{4,12},{8,0},{12,4},{1,9},{5,13},{9,1},{13,5},{2,10},{6,14},... | collective-permute-start | bytes 442376 | tf_op jit(solution)/shard_map/ppermute | solution.py:204
  47.3 24.3 %collective-permute-start.14 = (bf16[12,2,8,1024]{3,2,1,0:T(8,128)(2,1)S(1)}, bf16[12,2,8,1024]{3,2,1,0:T(8,128)(2,1)S(1)}, u32[]{:S(2)}, u32[]{:S(2)}) collective-permute-start(bf16[12,2,8,1024]{3,2,1,0:T(8,128)(2,1)S(1)} %get-tuple-element.230), channel_id=1, source_target_pairs={{0,4},{4,8},{8,12},{12,0},{1,5},{5,9},{9,13},{13,1},{2,6},{6,10},{... | collective-permute-start | bytes 1179656 | tf_op jit(solution)/shard_map/ppermute | solution.py:204
  47.9 15.3 %collective-permute-start.19 = (bf16[12,2,8,768]{3,2,1,0:T(8,128)(2,1)S(1)}, bf16[12,2,8,768]{3,2,1,0:T(8,128)(2,1)S(1)}, u32[]{:S(2)}, u32[]{:S(2)}) collective-permute-start(bf16[12,2,8,768]{3,2,1,0:T(8,128)(2,1)S(1)} %get-tuple-element.237), channel_id=1, source_target_pairs={{0,4},{4,8},{8,12},{12,0},{1,5},{5,9},{9,13},{13,1},{2,6},{6,10},{... | collective-permute-start | bytes 884744 | tf_op jit(solution)/shard_map/ppermute | solution.py:204
  48.4 22.6 %collective-permute-start.20 = (bf16[12,2,8,768]{3,2,1,0:T(8,128)(2,1)S(1)}, bf16[12,2,8,768]{3,2,1,0:T(8,128)(2,1)S(1)}, u32[]{:S(2)}, u32[]{:S(2)}) collective-permute-start(bf16[12,2,8,768]{3,2,1,0:T(8,128)(2,1)S(1)} %get-tuple-element.238), channel_id=1, source_target_pairs={{0,8},{4,12},{8,0},{12,4},{1,9},{5,13},{9,1},{13,5},{2,10},{6,14},... | collective-permute-start | bytes 884744 | tf_op jit(solution)/shard_map/ppermute | solution.py:204
  49.2 22.5 %collective-permute-start.21 = (bf16[12,2,8,768]{3,2,1,0:T(8,128)(2,1)S(1)}, bf16[12,2,8,768]{3,2,1,0:T(8,128)(2,1)S(1)}, u32[]{:S(2)}, u32[]{:S(2)}) collective-permute-start(bf16[12,2,8,768]{3,2,1,0:T(8,128)(2,1)S(1)} %get-tuple-element.239.prev_ref), channel_id=1, source_target_pairs={{0,12},{4,0},{8,4},{12,8},{1,13},{5,1},{9,5},{13,9},{2,14},{6,2},{... | collective-permute-start | bytes 884744 | tf_op jit(solution)/shard_map/ppermute | solution.py:204
  54.1 25.3 %collective-permute-start.15 = (bf16[12,2,8,1024]{3,2,1,0:T(8,128)(2,1)S(1)}, bf16[12,2,8,1024]{3,2,1,0:T(8,128)(2,1)S(1)}, u32[]{:S(2)}, u32[]{:S(2)}) collective-permute-start(bf16[12,2,8,1024]{3,2,1,0:T(8,128)(2,1)S(1)} %get-tuple-element.231), channel_id=1, source_target_pairs={{0,8},{4,12},{8,0},{12,4},{1,9},{5,13},{9,1},{13,5},{2,10},{6,14},... | collective-permute-start | bytes 1179656 | tf_op jit(solution)/shard_map/ppermute | solution.py:204
  63.1 38.8 %collective-permute-start.8 = (bf16[12,2,8,1152]{3,2,1,0:T(8,128)(2,1)S(1)}, bf16[12,2,8,1152]{3,2,1,0:T(8,128)(2,1)S(1)}, u32[]{:S(2)}, u32[]{:S(2)}) collective-permute-start(bf16[12,2,8,1152]{3,2,1,0:T(8,128)(2,1)S(1)} %get-tuple-element.223), channel_id=1, source_target_pairs={{0,4},{4,8},{8,12},{12,0},{1,5},{5,9},{9,13},{13,1},{2,6},{6,10},{... | collective-permute-start | bytes 1327112 | tf_op jit(solution)/shard_map/ppermute | solution.py:204
  71.0 31.8 %collective-permute-start.9 = (bf16[12,2,8,1152]{3,2,1,0:T(8,128)(2,1)S(1)}, bf16[12,2,8,1152]{3,2,1,0:T(8,128)(2,1)S(1)}, u32[]{:S(2)}, u32[]{:S(2)}) collective-permute-start(bf16[12,2,8,1152]{3,2,1,0:T(8,128)(2,1)S(1)} %get-tuple-element.224), channel_id=1, source_target_pairs={{0,8},{4,12},{8,0},{12,4},{1,9},{5,13},{9,1},{13,5},{2,10},{6,14},... | collective-permute-start | bytes 1327112 | tf_op jit(solution)/shard_map/ppermute | solution.py:204
  71.6 31.1 %collective-permute-start.10 = (bf16[12,2,8,1152]{3,2,1,0:T(8,128)(2,1)S(1)}, bf16[12,2,8,1152]{3,2,1,0:T(8,128)(2,1)S(1)}, u32[]{:S(2)}, u32[]{:S(2)}) collective-permute-start(bf16[12,2,8,1152]{3,2,1,0:T(8,128)(2,1)S(1)} %get-tuple-element.225.prev_ref), channel_id=1, source_target_pairs={{0,12},{4,0},{8,4},{12,8},{1,13},{5,1},{9,5},{13,9},{2,14},{6,2},{... | collective-permute-start | bytes 1327112 | tf_op jit(solution)/shard_map/ppermute | solution.py:204
  71.6 28.5 %collective-permute-start.16 = (bf16[12,2,8,1024]{3,2,1,0:T(8,128)(2,1)S(1)}, bf16[12,2,8,1024]{3,2,1,0:T(8,128)(2,1)S(1)}, u32[]{:S(2)}, u32[]{:S(2)}) collective-permute-start(bf16[12,2,8,1024]{3,2,1,0:T(8,128)(2,1)S(1)} %get-tuple-element.232.prev_ref), channel_id=1, source_target_pairs={{0,12},{4,0},{8,4},{12,8},{1,13},{5,1},{9,5},{13,9},{2,14},{6,2},{... | collective-permute-start | bytes 1179656 | tf_op jit(solution)/shard_map/ppermute | solution.py:204
  79.4 20.8 %collective-permute-start.6 = (bf16[8,2,8,640]{3,2,1,0:T(8,128)(2,1)S(1)}, bf16[8,2,8,640]{3,2,1,0:T(8,128)(2,1)S(1)}, u32[]{:S(2)}, u32[]{:S(2)}) collective-permute-start(bf16[8,2,8,640]{3,2,1,0:T(8,128)(2,1)S(1)} %get-tuple-element.220), channel_id=1, source_target_pairs={{0,1},{1,2},{2,3},{4,5},{5,6},{6,7},{8,9},{9,10},{10,11},{12,13},{... | collective-permute-start | bytes 491528 | tf_op jit(solution)/shard_map/ppermute | solution.py:20
  100.2 8.7 %collective-permute-start.26 = (bf16[12,2,8,384]{3,2,1,0:T(8,128)(2,1)S(1)}, bf16[12,2,8,384]{3,2,1,0:T(8,128)(2,1)S(1)}, u32[]{:S(2)}, u32[]{:S(2)}) collective-permute-start(bf16[12,2,8,384]{3,2,1,0:T(8,128)(2,1)S(1)} %get-tuple-element.246.prev_ref), channel_id=1, source_target_pairs={{0,12},{4,0},{8,4},{12,8},{1,13},{5,1},{9,5},{13,9},{2,14},{6,2},{... | collective-permute-start | bytes 442376 | tf_op jit(solution)/shard_map/ppermute | solution.py:204
  100.2 10.1 %collective-permute-start.29 = (bf16[12,2,8,256]{3,2,1,0:T(8,128)(2,1)S(1)}, bf16[12,2,8,256]{3,2,1,0:T(8,128)(2,1)S(1)}, u32[]{:S(2)}, u32[]{:S(2)}) collective-permute-start(bf16[12,2,8,256]{3,2,1,0:T(8,128)(2,1)S(1)} %get-tuple-element.251), channel_id=1, source_target_pairs={{0,4},{4,8},{8,12},{12,0},{1,5},{5,9},{9,13},{13,1},{2,6},{6,10},{... | collective-permute-start | bytes 294920 | tf_op jit(solution)/shard_map/ppermute | solution.py:204
  102.8 13.1 %collective-permute-start.7 = (bf16[8,2,8,640]{3,2,1,0:T(8,128)(2,1)S(1)}, bf16[8,2,8,640]{3,2,1,0:T(8,128)(2,1)S(1)}, u32[]{:S(2)}, u32[]{:S(2)}) collective-permute-start(bf16[8,2,8,640]{3,2,1,0:T(8,128)(2,1)S(1)} %get-tuple-element.221.refs_4_), channel_id=1, source_target_pairs={{1,0},{2,1},{3,2},{5,4},{6,5},{7,6},{9,8},{10,9},{11,10},{13,12},{... | collective-permute-start | bytes 491528 | tf_op jit(solution)/shard_map/ppermute | solution.py:20
  111.6 12.1 %collective-permute-start.32 = (bf16[8,2,8,256]{3,2,1,0:T(8,128)(2,1)S(1)}, bf16[8,2,8,256]{3,2,1,0:T(8,128)(2,1)S(1)}, u32[]{:S(2)}, u32[]{:S(2)}) collective-permute-start(bf16[8,2,8,256]{3,2,1,0:T(8,128)(2,1)S(1)} %get-tuple-element.255), channel_id=1, source_target_pairs={{0,1},{1,2},{2,3},{4,5},{5,6},{6,7},{8,9},{9,10},{10,11},{12,13},{... | collective-permute-start | bytes 196616 | tf_op jit(solution)/shard_map/ppermute | solution.py:20
  116.0 62.1 %collective-permute-start.34 = (bf16[16,2,8,128]{3,2,1,0:T(8,128)(2,1)S(1)}, bf16[16,2,8,128]{3,2,1,0:T(8,128)(2,1)S(1)}, u32[]{:S(2)}, u32[]{:S(2)}) collective-permute-start(bf16[16,2,8,128]{3,2,1,0:T(8,128)(2,1)S(1)} %slice.524), channel_id=1, source_target_pairs={{4,0},{8,4},{12,8},{5,1},{9,5},{13,9},{6,2},{10,6},{14,10},{7,3},{... | collective-permute-start | bytes 196616 | tf_op jit(solution)/shard_map/ppermute | solution.py:20
  119.9 52.3 %collective-permute-start.12 = (bf16[8,2,8,1152]{3,2,1,0:T(8,128)(2,1)S(1)}, bf16[8,2,8,1152]{3,2,1,0:T(8,128)(2,1)S(1)}, u32[]{:S(2)}, u32[]{:S(2)}) collective-permute-start(bf16[8,2,8,1152]{3,2,1,0:T(8,128)(2,1)S(1)} %get-tuple-element.228.refs_4_), channel_id=1, source_target_pairs={{1,0},{2,1},{3,2},{5,4},{6,5},{7,6},{9,8},{10,9},{11,10},{13,12},{... | collective-permute-start | bytes 884744 | tf_op jit(solution)/shard_map/ppermute | solution.py:20
  121.2 45.1 %collective-permute-start.18 = (bf16[8,2,8,1024]{3,2,1,0:T(8,128)(2,1)S(1)}, bf16[8,2,8,1024]{3,2,1,0:T(8,128)(2,1)S(1)}, u32[]{:S(2)}, u32[]{:S(2)}) collective-permute-start(bf16[8,2,8,1024]{3,2,1,0:T(8,128)(2,1)S(1)} %get-tuple-element.235.refs_4_), channel_id=1, source_target_pairs={{1,0},{2,1},{3,2},{5,4},{6,5},{7,6},{9,8},{10,9},{11,10},{13,12},{... | collective-permute-start | bytes 786440 | tf_op jit(solution)/shard_map/ppermute | solution.py:20
  122.5 40.3 %collective-permute-start.23 = (bf16[8,2,8,768]{3,2,1,0:T(8,128)(2,1)S(1)}, bf16[8,2,8,768]{3,2,1,0:T(8,128)(2,1)S(1)}, u32[]{:S(2)}, u32[]{:S(2)}) collective-permute-start(bf16[8,2,8,768]{3,2,1,0:T(8,128)(2,1)S(1)} %get-tuple-element.242.refs_4_), channel_id=1, source_target_pairs={{1,0},{2,1},{3,2},{5,4},{6,5},{7,6},{9,8},{10,9},{11,10},{13,12},{... | collective-permute-start | bytes 589832 | tf_op jit(solution)/shard_map/ppermute | solution.py:20
  123.8 17.9 %collective-permute-start.33 = (bf16[8,2,8,256]{3,2,1,0:T(8,128)(2,1)S(1)}, bf16[8,2,8,256]{3,2,1,0:T(8,128)(2,1)S(1)}, u32[]{:S(2)}, u32[]{:S(2)}) collective-permute-start(bf16[8,2,8,256]{3,2,1,0:T(8,128)(2,1)S(1)} %get-tuple-element.256), channel_id=1, source_target_pairs={{1,0},{2,1},{3,2},{5,4},{6,5},{7,6},{9,8},{10,9},{11,10},{13,12},{... | collective-permute-start | bytes 196616 | tf_op jit(solution)/shard_map/ppermute | solution.py:20
  162.8 9.3 %collective-permute-start.11 = (bf16[8,2,8,1152]{3,2,1,0:T(8,128)(2,1)S(1)}, bf16[8,2,8,1152]{3,2,1,0:T(8,128)(2,1)S(1)}, u32[]{:S(2)}, u32[]{:S(2)}) collective-permute-start(bf16[8,2,8,1152]{3,2,1,0:T(8,128)(2,1)S(1)} %get-tuple-element.227), channel_id=1, source_target_pairs={{0,1},{1,2},{2,3},{4,5},{5,6},{6,7},{8,9},{9,10},{10,11},{12,13},{... | collective-permute-start | bytes 884744 | tf_op jit(solution)/shard_map/ppermute | solution.py:20
  (13 other events, 69.5 us)
where the time goes:
time: 183 us; the launch traced here: 181 us
  waiting for transfers between devices  76.4 us (42%)
  starting transfers between devices  57 us (31%)
  Pallas kernels  39.2 us (21%)
  other arithmetic  4.38 us (2%)
  local copies, waits for them, and re-layouts  3.65 us (2%)
    ppermute x14, starting transfers between devices, shifted(): lax.ppermute(value, axis, [(source, source + steps) for source in range(f...  38.7 us
    ppermute x18, waiting for transfers between devices, local_body(): lax.ppermute(send_buf[step], 'skyx', rings[step])  37.1 us
    ppermute x14, waiting for transfers between devices, shifted(): lax.ppermute(value, axis, [(source, source + steps) for source in range(f...  32.6 us
    pallas_call x6, Pallas kernels, warp_chunk(): pl.pallas_call(make_warp_kernel(start, window, first_tile, exposures, gro...  30.3 us
    ppermute x18, starting transfers between devices, local_body(): lax.ppermute(send_buf[step], 'skyx', rings[step])  16.3 us
    pallas_call x6, Pallas kernels, place(): pl.pallas_call(make_place_kernel(groups, capacity, positions, margin, inn...  8.91 us
    ppermute x3, waiting for transfers between devices, local_body(): lax.ppermute(send_rows[step], 'skyx', rings[step])  6.69 us
  transfers between devices with their start and end apart: 35, of which 14 were waited for; matrix products, arithmetic and copies ran while one was open for 1% of the time, Pallas kernels for 19%

commit v1 on v0

--- a/solution.py
+++ b/solution.py
@@ -9,8 +9,8 @@
 OVY = 64
 PR = 128
 RB = 8
-SPLIT = (5, 8, 6, 3, 2, 9)
-ORDER = (0, 5, 1, 2, 3, 4)
+SPLIT = (5, 10, 9, 9)
+ORDER = (0, 3, 1, 2)
 ROW_PIECE = 640
 
 
@@ -24,7 +24,7 @@
     def kernel(w_ref, idx_ref, img_hbm, mask_hbm, rk_ref, ck_hbm, prev_ref, *refs):
         out_refs = refs[:groups]
         img_buf, mask_buf, rw_buf, blk_buf, ck_ref, sems = refs[groups:]
-        ph = rk_ref.shape[2]
+        ph = rk_ref.shape[3]
         tiles, kw, tw = ck_ref.shape
         blocks = ph // RB
         ck_copy = pltpu.make_async_copy(ck_hbm.at[pl.ds(first_tile, tiles)], ck_ref, sems.at[2, 0])
@@ -51,8 +51,12 @@
                 img = img_buf[e, :, cols]
                 p0 = jnp.where(good, img, jnp.zeros_like(img))
                 p1 = good.astype(jnp.bfloat16)
-                rw_buf[0:ph, cols] = jnp.dot(rk, p0, preferred_element_type=jnp.float32).astype(jnp.bfloat16)
-                rw_buf[ph : 2 * ph, cols] = jnp.dot(rk, p1, preferred_element_type=jnp.float32).astype(jnp.bfloat16)
+                rw_buf[0:ph, cols] = lax.dot_general(
+                    rk, p0, (((0,), (0,)), ((), ())), preferred_element_type=jnp.float32
+                ).astype(jnp.bfloat16)
+                rw_buf[ph : 2 * ph, cols] = lax.dot_general(
+                    rk, p1, (((0,), (0,)), ((), ())), preferred_element_type=jnp.float32
+                ).astype(jnp.bfloat16)
                 piece_start += piece
             weight = w_ref[e]
 
@@ -114,7 +118,7 @@
             transcendentals=0,
             bytes_accessed=exposures * hin * window * 6 + per * kw * tw * 2 + slots * 2 * RB * width * 2,
         ),
-    )(weights, send_idx, images, masks, row_kernels, col_kernel, previous)
+    )(weights, send_idx, images, masks, jnp.swapaxes(row_kernels, 2, 3), col_kernel, previous)
 
 
 def make_place_kernel(groups, capacity, positions, margin, inner):

time: 183 us -> 108 us (0.59)
  waiting for transfers between devices: 76.4 us -> 31.7 us
  starting transfers between devices: 57 us -> 34.3 us
  Pallas kernels: 39.2 us -> 32.5 us
    ppermute x14 -> x10, waiting for transfers between devices: 32.6 us -> 7.13 us  [shifted(): lax.ppermute(value, axis, [(source, source + steps) for source in range(f...]
    ppermute x14 -> x10, starting transfers between devices: 38.7 us -> 21.6 us  [shifted(): lax.ppermute(value, axis, [(source, source + steps) for source in range(f...]
    ppermute x18 -> x12, waiting for transfers between devices: 37.1 us -> 22.6 us  [local_body(): lax.ppermute(send_buf[step], 'skyx', rings[step])]
    ppermute x18 -> x12, starting transfers between devices: 16.3 us -> 11.3 us  [local_body(): lax.ppermute(send_buf[step], 'skyx', rings[step])]
    ppermute x3, waiting for transfers between devices: 6.69 us -> 1.96 us  [local_body(): lax.ppermute(send_rows[step], 'skyx', rings[step])]
    pallas_call x6 -> x4, Pallas kernels: 30.3 us -> 26.1 us  [warp_chunk(): pl.pallas_call(make_warp_kernel(start, window, first_tile, exposures, gro...]
    pallas_call x6 -> x4, Pallas kernels: 8.91 us -> 6.41 us  [place(): pl.pallas_call(make_place_kernel(groups, capacity, positions, margin, inn...]
  transfers between devices with their start and end apart: 35 -> 25, of which waited for: 14 -> 9; matrix products, arithmetic and copies ran while one was open for 1% -> 1% of each run, Pallas kernels for 19% -> 26%
where the time goes in v1:
time: 108 us; the launch traced here: 107 us
  starting transfers between devices  34.3 us (32%)
  Pallas kernels  32.5 us (30%)
  waiting for transfers between devices  31.7 us (29%)
  other arithmetic  4.59 us (4%)
  local copies, waits for them, and re-layouts  3.24 us (3%)
    pallas_call x4, Pallas kernels, warp_chunk(): pl.pallas_call(make_warp_kernel(start, window, first_tile, exposures, gro...  26.1 us
    ppermute x12, waiting for transfers between devices, local_body(): lax.ppermute(send_buf[step], 'skyx', rings[step])  22.6 us
    ppermute x10, starting transfers between devices, shifted(): lax.ppermute(value, axis, [(source, source + steps) for source in range(f...  21.6 us
    ppermute x12, starting transfers between devices, local_body(): lax.ppermute(send_buf[step], 'skyx', rings[step])  11.3 us
    ppermute x10, waiting for transfers between devices, shifted(): lax.ppermute(value, axis, [(source, source + steps) for source in range(f...  7.13 us
    pallas_call x4, Pallas kernels, place(): pl.pallas_call(make_place_kernel(groups, capacity, positions, margin, inn...  6.41 us
    unnamed x6, local copies, waits for them, and re-layouts  2.58 us
  transfers between devices with their start and end apart: 25, of which 9 were waited for; matrix products, arithmetic and copies ran while one was open for 1% of the time, Pallas kernels for 26%

profile of v1, /device:TPU:1, one launch (start us, length us, event | category | flops | bytes accessed | tf_op | source)
XLA Modules:
  0.0 106.9 jit_solution(972196028917379581)
XLA Ops:
  2.3 1.7 %copy-done.1 = bf16[1,2,136,4480]{3,2,1,0:T(8,128)(2,1)S(1)} copy-done((bf16[1,2,136,4480]{3,2,1,0:T(8,128)(2,1)S(1)}, bf16[1,2,136,4480]{3,2,1,0:T(8,128)(2,1)}, u32[]{:S(2)}) %copy-start.1) | copy-done | bytes 2437144
  4.8 4.9 %shard_map.73 = (bf16[12,2,8,640]{3,2,1,0:T(8,128)(2,1)S(1)}, bf16[12,2,8,640]{3,2,1,0:T(8,128)(2,1)S(1)}, bf16[12,2,8,640]{3,2,1,0:T(8,128)(2,1)S(1)}, bf16[12,2,8,640]{3,2,1,0:T(8,128)(2,1)S(1)}) custom-call(f32[2]{0:T(128)S(1)} %fusion.13.w_ref, s32[48]{0:T(128)S(1)} %min.12.idx_ref.prev_ref, bf16[1,2,136,4480]{3,2,1,0:T(8,128)(2,1)S(1)} %copy-done.1, ...), custom_call_target="tpu_custom_call" | custom-call | flops 501219328 | bytes 2936832 | tf_op jit(solution)/shard_map/pallas_call | solution.py:94
  9.7 2.7 %collective-permute-start.3 = (bf16[12,2,8,640]{3,2,1,0:T(8,128)(2,1)S(1)}, bf16[12,2,8,640]{3,2,1,0:T(8,128)(2,1)S(1)}, u32[]{:S(2)}, u32[]{:S(2)}) collective-permute-start(bf16[12,2,8,640]{3,2,1,0:T(8,128)(2,1)S(1)} %get-tuple-element.154), channel_id=1, source_target_pairs={{0,4},{4,8},{8,12},{12,0},{1,5},{5,9},{9,13},{13,1},{2,6},{6,10},{... | collective-permute-start | bytes 737288 | tf_op jit(solution)/shard_map/ppermute | solution.py:208
  14.5 6.9 %shard_map.75 = (bf16[12,2,8,1152]{3,2,1,0:T(8,128)(2,1)S(1)}, bf16[12,2,8,1152]{3,2,1,0:T(8,128)(2,1)S(1)}, bf16[12,2,8,1152]{3,2,1,0:T(8,128)(2,1)S(1)}, bf16[12,2,8,1152]{3,2,1,0:T(8,128)(2,1)S(1)}) custom-call(f32[2]{0:T(128)S(1)} %fusion.13.w_ref, s32[48]{0:T(128)S(1)} %min.12.idx_ref.prev_ref, bf16[1,2,136,4480]{3,2,1,0:T(8,128)(2,1)S(1)} %copy-done.1, ...), custom_call_target="tpu_custom_call" | custom-call | flops 845152256 | bytes 4952064 | tf_op jit(solution)/shard_map/pallas_call | solution.py:94
  21.4 2.0 %collective-permute-done.2 = s32[12]{0:T(128)S(1)} collective-permute-done((s32[12]{0:T(128)S(1)}, s32[12]{0:T(128)S(1)}, u32[]{:S(2)}, u32[]{:S(2)}) %collective-permute-start.2) | collective-permute-done | bytes 80 | tf_op jit(solution)/shard_map/ppermute | solution.py:195
  23.4 2.5 %collective-permute-start.8 = (bf16[12,2,8,1152]{3,2,1,0:T(8,128)(2,1)S(1)}, bf16[12,2,8,1152]{3,2,1,0:T(8,128)(2,1)S(1)}, u32[]{:S(2)}, u32[]{:S(2)}) collective-permute-start(bf16[12,2,8,1152]{3,2,1,0:T(8,128)(2,1)S(1)} %get-tuple-element.161), channel_id=1, source_target_pairs={{0,4},{4,8},{8,12},{12,0},{1,5},{5,9},{9,13},{13,1},{2,6},{6,10},{... | collective-permute-start | bytes 1327112 | tf_op jit(solution)/shard_map/ppermute | solution.py:208
  27.1 7.4 %shard_map.77 = (bf16[12,2,8,1280]{3,2,1,0:T(8,128)(2,1)S(1)}, bf16[12,2,8,1280]{3,2,1,0:T(8,128)(2,1)S(1)}, bf16[12,2,8,1280]{3,2,1,0:T(8,128)(2,1)S(1)}, bf16[12,2,8,1280]{3,2,1,0:T(8,128)(2,1)S(1)}) custom-call(f32[2]{0:T(128)S(1)} %fusion.13.w_ref, s32[48]{0:T(128)S(1)} %min.12.idx_ref.prev_ref, bf16[1,2,136,4480]{3,2,1,0:T(8,128)(2,1)S(1)} %copy-done.1, ...), custom_call_target="tpu_custom_call" | custom-call | flops 931135488 | bytes 5455872 | tf_op jit(solution)/shard_map/pallas_call | solution.py:94
  34.5 1.7 %collective-permute-start.14 = (bf16[12,2,8,1280]{3,2,1,0:T(8,128)(2,1)S(1)}, bf16[12,2,8,1280]{3,2,1,0:T(8,128)(2,1)S(1)}, u32[]{:S(2)}, u32[]{:S(2)}) collective-permute-start(bf16[12,2,8,1280]{3,2,1,0:T(8,128)(2,1)S(1)} %get-tuple-element.168), channel_id=1, source_target_pairs={{0,4},{4,8},{8,12},{12,0},{1,5},{5,9},{9,13},{13,1},{2,6},{6,10},{... | collective-permute-start | bytes 1474568 | tf_op jit(solution)/shard_map/ppermute | solution.py:208
  38.2 3.2 %collective-permute-start.6 = (bf16[8,2,8,640]{3,2,1,0:T(8,128)(2,1)S(1)}, bf16[8,2,8,640]{3,2,1,0:T(8,128)(2,1)S(1)}, u32[]{:S(2)}, u32[]{:S(2)}) collective-permute-start(bf16[8,2,8,640]{3,2,1,0:T(8,128)(2,1)S(1)} %get-tuple-element.158), channel_id=1, source_target_pairs={{0,1},{1,2},{2,3},{4,5},{5,6},{6,7},{8,9},{9,10},{10,11},{12,13},{... | collective-permute-start | bytes 491528 | tf_op jit(solution)/shard_map/ppermute | solution.py:20
  41.4 2.6 %collective-permute-done.9.refs_2_ = bf16[12,2,8,1152]{3,2,1,0:T(8,128)(2,1)S(1)} collective-permute-done((bf16[12,2,8,1152]{3,2,1,0:T(8,128)(2,1)S(1)}, bf16[12,2,8,1152]{3,2,1,0:T(8,128)(2,1)S(1)}, u32[]{:S(2)}, u32[]{:S(2)}) %collective-permute-start.9) | collective-permute-done | bytes 442400 | tf_op jit(solution)/shard_map/ppermute | solution.py:208
  45.3 3.9 %collective-permute-done.10.refs_3_ = bf16[12,2,8,1152]{3,2,1,0:T(8,128)(2,1)S(1)} collective-permute-done((bf16[12,2,8,1152]{3,2,1,0:T(8,128)(2,1)S(1)}, bf16[12,2,8,1152]{3,2,1,0:T(8,128)(2,1)S(1)}, u32[]{:S(2)}, u32[]{:S(2)}) %collective-permute-start.10) | collective-permute-done | bytes 442400 | tf_op jit(solution)/shard_map/ppermute | solution.py:208
  49.2 6.9 %shard_map.79 = (bf16[12,2,8,1152]{3,2,1,0:T(8,128)(2,1)S(1)}, bf16[12,2,8,1152]{3,2,1,0:T(8,128)(2,1)S(1)}, bf16[12,2,8,1152]{3,2,1,0:T(8,128)(2,1)S(1)}, bf16[12,2,8,1152]{3,2,1,0:T(8,128)(2,1)S(1)}) custom-call(f32[2]{0:T(128)S(1)} %fusion.13.w_ref, s32[48]{0:T(128)S(1)} %min.12.idx_ref.prev_ref, bf16[1,2,136,4480]{3,2,1,0:T(8,128)(2,1)S(1)} %copy-done.1, ...), custom_call_target="tpu_custom_call" | custom-call | flops 845152256 | bytes 4952064 | tf_op jit(solution)/shard_map/pallas_call | solution.py:94
  57.8 1.9 %collective-permute-start.19 = (bf16[12,2,8,1152]{3,2,1,0:T(8,128)(2,1)S(1)}, bf16[12,2,8,1152]{3,2,1,0:T(8,128)(2,1)S(1)}, u32[]{:S(2)}, u32[]{:S(2)}) collective-permute-start(bf16[12,2,8,1152]{3,2,1,0:T(8,128)(2,1)S(1)} %get-tuple-element.175), channel_id=1, source_target_pairs={{0,4},{4,8},{8,12},{12,0},{1,5},{5,9},{9,13},{13,1},{2,6},{6,10},{... | collective-permute-start | bytes 1327112 | tf_op jit(solution)/shard_map/ppermute | solution.py:208
  60.1 5.0 %collective-permute-done.15.refs_2_ = bf16[12,2,8,1280]{3,2,1,0:T(8,128)(2,1)S(1)} collective-permute-done((bf16[12,2,8,1280]{3,2,1,0:T(8,128)(2,1)S(1)}, bf16[12,2,8,1280]{3,2,1,0:T(8,128)(2,1)S(1)}, u32[]{:S(2)}, u32[]{:S(2)}) %collective-permute-start.15) | collective-permute-done | bytes 491552 | tf_op jit(solution)/shard_map/ppermute | solution.py:208
  65.1 2.7 %collective-permute-start.11 = (bf16[8,2,8,1152]{3,2,1,0:T(8,128)(2,1)S(1)}, bf16[8,2,8,1152]{3,2,1,0:T(8,128)(2,1)S(1)}, u32[]{:S(2)}, u32[]{:S(2)}) collective-permute-start(bf16[8,2,8,1152]{3,2,1,0:T(8,128)(2,1)S(1)} %get-tuple-element.165), channel_id=1, source_target_pairs={{0,1},{1,2},{2,3},{4,5},{5,6},{6,7},{8,9},{9,10},{10,11},{12,13},{... | collective-permute-start | bytes 884744 | tf_op jit(solution)/shard_map/ppermute | solution.py:20
  68.0 2.2 %collective-permute-done.16.refs_3_ = bf16[12,2,8,1280]{3,2,1,0:T(8,128)(2,1)S(1)} collective-permute-done((bf16[12,2,8,1280]{3,2,1,0:T(8,128)(2,1)S(1)}, bf16[12,2,8,1280]{3,2,1,0:T(8,128)(2,1)S(1)}, u32[]{:S(2)}, u32[]{:S(2)}) %collective-permute-start.16) | collective-permute-done | bytes 491552 | tf_op jit(solution)/shard_map/ppermute | solution.py:208
  70.3 1.9 %collective-permute-start.24 = (bf16[16,2,8,128]{3,2,1,0:T(8,128)(2,1)S(1)}, bf16[16,2,8,128]{3,2,1,0:T(8,128)(2,1)S(1)}, u32[]{:S(2)}, u32[]{:S(2)}) collective-permute-start(bf16[16,2,8,128]{3,2,1,0:T(8,128)(2,1)S(1)} %slice.394), channel_id=1, source_target_pairs={{4,0},{8,4},{12,8},{5,1},{9,5},{13,9},{6,2},{10,6},{14,10},{7,3},{... | collective-permute-start | bytes 196616 | tf_op jit(solution)/shard_map/ppermute | solution.py:20
  72.2 1.7 %shard_map.78 = (bf16[8,2,8,1280]{3,2,1,0:T(8,128)(2,1)S(1)}, bf16[8,2,8,1280]{3,2,1,0:T(8,128)(2,1)S(1)}, f32[16,2,8,1280]{3,2,1,0:T(8,128)S(1)}) custom-call(s32[48]{0:T(128)S(1)} %pad_add_fusion.rows_ref.refs_4_, bf16[12,2,8,1280]{3,2,1,0:T(8,128)(2,1)S(1)} %get-tuple-element.167.refs_0_, bf16[12,2,8,1280]{3,2,1,0:T(8,128)(2,1)S(1)} %collective-permute-done.14.refs_1_, ...), custom_call_target="tpu_custom_call" | custom-call | tf_op jit(solution)/shard_map/pallas_call | solution.py:152
  75.9 8.2 %collective-permute-done.20.refs_2_ = bf16[12,2,8,1152]{3,2,1,0:T(8,128)(2,1)S(1)} collective-permute-done((bf16[12,2,8,1152]{3,2,1,0:T(8,128)(2,1)S(1)}, bf16[12,2,8,1152]{3,2,1,0:T(8,128)(2,1)S(1)}, u32[]{:S(2)}, u32[]{:S(2)}) %collective-permute-start.20) | collective-permute-done | bytes 442400 | tf_op jit(solution)/shard_map/ppermute | solution.py:208
  84.1 2.7 %collective-permute-start.17 = (bf16[8,2,8,1280]{3,2,1,0:T(8,128)(2,1)S(1)}, bf16[8,2,8,1280]{3,2,1,0:T(8,128)(2,1)S(1)}, u32[]{:S(2)}, u32[]{:S(2)}) collective-permute-start(bf16[8,2,8,1280]{3,2,1,0:T(8,128)(2,1)S(1)} %get-tuple-element.172), channel_id=1, source_target_pairs={{0,1},{1,2},{2,3},{4,5},{5,6},{6,7},{8,9},{9,10},{10,11},{12,13},{... | collective-permute-start | bytes 983048 | tf_op jit(solution)/shard_map/ppermute | solution.py:20
  89.8 4.0 %collective-permute-start.22 = (bf16[8,2,8,1152]{3,2,1,0:T(8,128)(2,1)S(1)}, bf16[8,2,8,1152]{3,2,1,0:T(8,128)(2,1)S(1)}, u32[]{:S(2)}, u32[]{:S(2)}) collective-permute-start(bf16[8,2,8,1152]{3,2,1,0:T(8,128)(2,1)S(1)} %get-tuple-element.179), channel_id=1, source_target_pairs={{0,1},{1,2},{2,3},{4,5},{5,6},{6,7},{8,9},{9,10},{10,11},{12,13},{... | collective-permute-start | bytes 884744 | tf_op jit(solution)/shard_map/ppermute | solution.py:20
  95.5 1.9 %collective-permute-start.13 = (bf16[16,2,8,128]{3,2,1,0:T(8,128)(2,1)S(1)}, bf16[16,2,8,128]{3,2,1,0:T(8,128)(2,1)S(1)}, u32[]{:S(2)}, u32[]{:S(2)}) collective-permute-start(bf16[16,2,8,128]{3,2,1,0:T(8,128)(2,1)S(1)} %slice.395), channel_id=1, source_target_pairs={{0,4},{4,8},{8,12},{1,5},{5,9},{9,13},{2,6},{6,10},{10,14},{3,7},{... | collective-permute-start | bytes 196616 | tf_op jit(solution)/shard_map/ppermute | solution.py:20
  97.4 3.2 %collective-permute-done.22 = bf16[8,2,8,1152]{3,2,1,0:T(8,128)(2,1)S(1)} collective-permute-done((bf16[8,2,8,1152]{3,2,1,0:T(8,128)(2,1)S(1)}, bf16[8,2,8,1152]{3,2,1,0:T(8,128)(2,1)S(1)}, u32[]{:S(2)}, u32[]{:S(2)}) %collective-permute-start.22) | collective-permute-done | bytes 294944 | tf_op jit(solution)/shard_map/ppermute | solution.py:20
  100.7 4.0 %collective-permute-done.23 = bf16[8,2,8,1152]{3,2,1,0:T(8,128)(2,1)S(1)} collective-permute-done((bf16[8,2,8,1152]{3,2,1,0:T(8,128)(2,1)S(1)}, bf16[8,2,8,1152]{3,2,1,0:T(8,128)(2,1)S(1)}, u32[]{:S(2)}, u32[]{:S(2)}) %collective-permute-start.23) | collective-permute-done | bytes 294944 | tf_op jit(solution)/shard_map/ppermute | solution.py:20
  (69 shorter events, 20.9 us)
Async XLA Ops:
  9.7 16.9 %collective-permute-start.3 = (bf16[12,2,8,640]{3,2,1,0:T(8,128)(2,1)S(1)}, bf16[12,2,8,640]{3,2,1,0:T(8,128)(2,1)S(1)}, u32[]{:S(2)}, u32[]{:S(2)}) collective-permute-start(bf16[12,2,8,640]{3,2,1,0:T(8,128)(2,1)S(1)} %get-tuple-element.154), channel_id=1, source_target_pairs={{0,4},{4,8},{8,12},{12,0},{1,5},{5,9},{9,13},{13,1},{2,6},{6,10},{... | collective-permute-start | bytes 737288 | tf_op jit(solution)/shard_map/ppermute | solution.py:208
  12.4 22.1 %collective-permute-start.4 = (bf16[12,2,8,640]{3,2,1,0:T(8,128)(2,1)S(1)}, bf16[12,2,8,640]{3,2,1,0:T(8,128)(2,1)S(1)}, u32[]{:S(2)}, u32[]{:S(2)}) collective-permute-start(bf16[12,2,8,640]{3,2,1,0:T(8,128)(2,1)S(1)} %get-tuple-element.155), channel_id=1, source_target_pairs={{0,8},{4,12},{8,0},{12,4},{1,9},{5,13},{9,1},{13,5},{2,10},{6,14},... | collective-permute-start | bytes 737288 | tf_op jit(solution)/shard_map/ppermute | solution.py:208
  12.4 23.8 %collective-permute-start.5 = (bf16[12,2,8,640]{3,2,1,0:T(8,128)(2,1)S(1)}, bf16[12,2,8,640]{3,2,1,0:T(8,128)(2,1)S(1)}, u32[]{:S(2)}, u32[]{:S(2)}) collective-permute-start(bf16[12,2,8,640]{3,2,1,0:T(8,128)(2,1)S(1)} %get-tuple-element.156.prev_ref), channel_id=1, source_target_pairs={{0,12},{4,0},{8,4},{12,8},{1,13},{5,1},{9,5},{13,9},{2,14},{6,2},{... | collective-permute-start | bytes 737288 | tf_op jit(solution)/shard_map/ppermute | solution.py:208
  13.1 10.3 %collective-permute-start.2 = (s32[12]{0:T(128)S(1)}, s32[12]{0:T(128)S(1)}, u32[]{:S(2)}, u32[]{:S(2)}) collective-permute-start(s32[12]{0:T(128)S(1)} %get-tuple-element.182), channel_id=1, source_target_pairs={{0,12},{4,0},{8,4},{12,8},{1,13},{5,1},{9,5},{13,9},{2,14},{6,2},{... | collective-permute-start | bytes 152 | tf_op jit(solution)/shard_map/ppermute | solution.py:195
  14.5 8.9 %collective-permute-start.1 = (s32[12]{0:T(128)S(1)}, s32[12]{0:T(128)S(1)}, u32[]{:S(2)}, u32[]{:S(2)}) collective-permute-start(s32[12]{0:T(128)S(1)} %get-tuple-element.183), channel_id=1, source_target_pairs={{0,8},{4,12},{8,0},{12,4},{1,9},{5,13},{9,1},{13,5},{2,10},{6,14},... | collective-permute-start | bytes 152 | tf_op jit(solution)/shard_map/ppermute | solution.py:195
  23.4 14.8 %collective-permute-start.8 = (bf16[12,2,8,1152]{3,2,1,0:T(8,128)(2,1)S(1)}, bf16[12,2,8,1152]{3,2,1,0:T(8,128)(2,1)S(1)}, u32[]{:S(2)}, u32[]{:S(2)}) collective-permute-start(bf16[12,2,8,1152]{3,2,1,0:T(8,128)(2,1)S(1)} %get-tuple-element.161), channel_id=1, source_target_pairs={{0,4},{4,8},{8,12},{12,0},{1,5},{5,9},{9,13},{13,1},{2,6},{6,10},{... | collective-permute-start | bytes 1327112 | tf_op jit(solution)/shard_map/ppermute | solution.py:208
  25.9 18.1 %collective-permute-start.9 = (bf16[12,2,8,1152]{3,2,1,0:T(8,128)(2,1)S(1)}, bf16[12,2,8,1152]{3,2,1,0:T(8,128)(2,1)S(1)}, u32[]{:S(2)}, u32[]{:S(2)}) collective-permute-start(bf16[12,2,8,1152]{3,2,1,0:T(8,128)(2,1)S(1)} %get-tuple-element.162), channel_id=1, source_target_pairs={{0,8},{4,12},{8,0},{12,4},{1,9},{5,13},{9,1},{13,5},{2,10},{6,14},... | collective-permute-start | bytes 1327112 | tf_op jit(solution)/shard_map/ppermute | solution.py:208
  26.6 22.6 %collective-permute-start.10 = (bf16[12,2,8,1152]{3,2,1,0:T(8,128)(2,1)S(1)}, bf16[12,2,8,1152]{3,2,1,0:T(8,128)(2,1)S(1)}, u32[]{:S(2)}, u32[]{:S(2)}) collective-permute-start(bf16[12,2,8,1152]{3,2,1,0:T(8,128)(2,1)S(1)} %get-tuple-element.163.prev_ref), channel_id=1, source_target_pairs={{0,12},{4,0},{8,4},{12,8},{1,13},{5,1},{9,5},{13,9},{2,14},{6,2},{... | collective-permute-start | bytes 1327112 | tf_op jit(solution)/shard_map/ppermute | solution.py:208
  34.5 25.2 %collective-permute-start.14 = (bf16[12,2,8,1280]{3,2,1,0:T(8,128)(2,1)S(1)}, bf16[12,2,8,1280]{3,2,1,0:T(8,128)(2,1)S(1)}, u32[]{:S(2)}, u32[]{:S(2)}) collective-permute-start(bf16[12,2,8,1280]{3,2,1,0:T(8,128)(2,1)S(1)} %get-tuple-element.168), channel_id=1, source_target_pairs={{0,4},{4,8},{8,12},{12,0},{1,5},{5,9},{9,13},{13,1},{2,6},{6,10},{... | collective-permute-start | bytes 1474568 | tf_op jit(solution)/shard_map/ppermute | solution.py:208
  36.2 28.9 %collective-permute-start.15 = (bf16[12,2,8,1280]{3,2,1,0:T(8,128)(2,1)S(1)}, bf16[12,2,8,1280]{3,2,1,0:T(8,128)(2,1)S(1)}, u32[]{:S(2)}, u32[]{:S(2)}) collective-permute-start(bf16[12,2,8,1280]{3,2,1,0:T(8,128)(2,1)S(1)} %get-tuple-element.169), channel_id=1, source_target_pairs={{0,8},{4,12},{8,0},{12,4},{1,9},{5,13},{9,1},{13,5},{2,10},{6,14},... | collective-permute-start | bytes 1474568 | tf_op jit(solution)/shard_map/ppermute | solution.py:208
  38.2 19.6 %collective-permute-start.6 = (bf16[8,2,8,640]{3,2,1,0:T(8,128)(2,1)S(1)}, bf16[8,2,8,640]{3,2,1,0:T(8,128)(2,1)S(1)}, u32[]{:S(2)}, u32[]{:S(2)}) collective-permute-start(bf16[8,2,8,640]{3,2,1,0:T(8,128)(2,1)S(1)} %get-tuple-element.158), channel_id=1, source_target_pairs={{0,1},{1,2},{2,3},{4,5},{5,6},{6,7},{8,9},{9,10},{10,11},{12,13},{... | collective-permute-start | bytes 491528 | tf_op jit(solution)/shard_map/ppermute | solution.py:20
  44.1 15.6 %collective-permute-start.7 = (bf16[8,2,8,640]{3,2,1,0:T(8,128)(2,1)S(1)}, bf16[8,2,8,640]{3,2,1,0:T(8,128)(2,1)S(1)}, u32[]{:S(2)}, u32[]{:S(2)}) collective-permute-start(bf16[8,2,8,640]{3,2,1,0:T(8,128)(2,1)S(1)} %get-tuple-element.159.refs_4_), channel_id=1, source_target_pairs={{1,0},{2,1},{3,2},{5,4},{6,5},{7,6},{9,8},{10,9},{11,10},{13,12},{... | collective-permute-start | bytes 491528 | tf_op jit(solution)/shard_map/ppermute | solution.py:20
  49.2 21.1 %collective-permute-start.16 = (bf16[12,2,8,1280]{3,2,1,0:T(8,128)(2,1)S(1)}, bf16[12,2,8,1280]{3,2,1,0:T(8,128)(2,1)S(1)}, u32[]{:S(2)}, u32[]{:S(2)}) collective-permute-start(bf16[12,2,8,1280]{3,2,1,0:T(8,128)(2,1)S(1)} %get-tuple-element.170.prev_ref), channel_id=1, source_target_pairs={{0,12},{4,0},{8,4},{12,8},{1,13},{5,1},{9,5},{13,9},{2,14},{6,2},{... | collective-permute-start | bytes 1474568 | tf_op jit(solution)/shard_map/ppermute | solution.py:208
  57.8 16.8 %collective-permute-start.19 = (bf16[12,2,8,1152]{3,2,1,0:T(8,128)(2,1)S(1)}, bf16[12,2,8,1152]{3,2,1,0:T(8,128)(2,1)S(1)}, u32[]{:S(2)}, u32[]{:S(2)}) collective-permute-start(bf16[12,2,8,1152]{3,2,1,0:T(8,128)(2,1)S(1)} %get-tuple-element.175), channel_id=1, source_target_pairs={{0,4},{4,8},{8,12},{12,0},{1,5},{5,9},{9,13},{13,1},{2,6},{6,10},{... | collective-permute-start | bytes 1327112 | tf_op jit(solution)/shard_map/ppermute | solution.py:208
  59.7 24.4 %collective-permute-start.20 = (bf16[12,2,8,1152]{3,2,1,0:T(8,128)(2,1)S(1)}, bf16[12,2,8,1152]{3,2,1,0:T(8,128)(2,1)S(1)}, u32[]{:S(2)}, u32[]{:S(2)}) collective-permute-start(bf16[12,2,8,1152]{3,2,1,0:T(8,128)(2,1)S(1)} %get-tuple-element.176), channel_id=1, source_target_pairs={{0,8},{4,12},{8,0},{12,4},{1,9},{5,13},{9,1},{13,5},{2,10},{6,14},... | collective-permute-start | bytes 1327112 | tf_op jit(solution)/shard_map/ppermute | solution.py:208
  59.7 27.1 %collective-permute-start.21 = (bf16[12,2,8,1152]{3,2,1,0:T(8,128)(2,1)S(1)}, bf16[12,2,8,1152]{3,2,1,0:T(8,128)(2,1)S(1)}, u32[]{:S(2)}, u32[]{:S(2)}) collective-permute-start(bf16[12,2,8,1152]{3,2,1,0:T(8,128)(2,1)S(1)} %get-tuple-element.177), channel_id=1, source_target_pairs={{0,12},{4,0},{8,4},{12,8},{1,13},{5,1},{9,5},{13,9},{2,14},{6,2},{... | collective-permute-start | bytes 1327112 | tf_op jit(solution)/shard_map/ppermute | solution.py:208
  65.1 24.6 %collective-permute-start.11 = (bf16[8,2,8,1152]{3,2,1,0:T(8,128)(2,1)S(1)}, bf16[8,2,8,1152]{3,2,1,0:T(8,128)(2,1)S(1)}, u32[]{:S(2)}, u32[]{:S(2)}) collective-permute-start(bf16[8,2,8,1152]{3,2,1,0:T(8,128)(2,1)S(1)} %get-tuple-element.165), channel_id=1, source_target_pairs={{0,1},{1,2},{2,3},{4,5},{5,6},{6,7},{8,9},{9,10},{10,11},{12,13},{... | collective-permute-start | bytes 884744 | tf_op jit(solution)/shard_map/ppermute | solution.py:20
  70.3 25.2 %collective-permute-start.24 = (bf16[16,2,8,128]{3,2,1,0:T(8,128)(2,1)S(1)}, bf16[16,2,8,128]{3,2,1,0:T(8,128)(2,1)S(1)}, u32[]{:S(2)}, u32[]{:S(2)}) collective-permute-start(bf16[16,2,8,128]{3,2,1,0:T(8,128)(2,1)S(1)} %slice.394), channel_id=1, source_target_pairs={{4,0},{8,4},{12,8},{5,1},{9,5},{13,9},{6,2},{10,6},{14,10},{7,3},{... | collective-permute-start | bytes 196616 | tf_op jit(solution)/shard_map/ppermute | solution.py:20
  74.6 19.3 %collective-permute-start.12 = (bf16[8,2,8,1152]{3,2,1,0:T(8,128)(2,1)S(1)}, bf16[8,2,8,1152]{3,2,1,0:T(8,128)(2,1)S(1)}, u32[]{:S(2)}, u32[]{:S(2)}) collective-permute-start(bf16[8,2,8,1152]{3,2,1,0:T(8,128)(2,1)S(1)} %get-tuple-element.166.refs_4_), channel_id=1, source_target_pairs={{1,0},{2,1},{3,2},{5,4},{6,5},{7,6},{9,8},{10,9},{11,10},{13,12},{... | collective-permute-start | bytes 884744 | tf_op jit(solution)/shard_map/ppermute | solution.py:20
  84.1 20.7 %collective-permute-start.17 = (bf16[8,2,8,1280]{3,2,1,0:T(8,128)(2,1)S(1)}, bf16[8,2,8,1280]{3,2,1,0:T(8,128)(2,1)S(1)}, u32[]{:S(2)}, u32[]{:S(2)}) collective-permute-start(bf16[8,2,8,1280]{3,2,1,0:T(8,128)(2,1)S(1)} %get-tuple-element.172), channel_id=1, source_target_pairs={{0,1},{1,2},{2,3},{4,5},{5,6},{6,7},{8,9},{9,10},{10,11},{12,13},{... | collective-permute-start | bytes 983048 | tf_op jit(solution)/shard_map/ppermute | solution.py:20
  86.8 18.1 %collective-permute-start.18 = (bf16[8,2,8,1280]{3,2,1,0:T(8,128)(2,1)S(1)}, bf16[8,2,8,1280]{3,2,1,0:T(8,128)(2,1)S(1)}, u32[]{:S(2)}, u32[]{:S(2)}) collective-permute-start(bf16[8,2,8,1280]{3,2,1,0:T(8,128)(2,1)S(1)} %get-tuple-element.173.refs_4_), channel_id=1, source_target_pairs={{1,0},{2,1},{3,2},{5,4},{6,5},{7,6},{9,8},{10,9},{11,10},{13,12},{... | collective-permute-start | bytes 983048 | tf_op jit(solution)/shard_map/ppermute | solution.py:20
  89.8 10.8 %collective-permute-start.22 = (bf16[8,2,8,1152]{3,2,1,0:T(8,128)(2,1)S(1)}, bf16[8,2,8,1152]{3,2,1,0:T(8,128)(2,1)S(1)}, u32[]{:S(2)}, u32[]{:S(2)}) collective-permute-start(bf16[8,2,8,1152]{3,2,1,0:T(8,128)(2,1)S(1)} %get-tuple-element.179), channel_id=1, source_target_pairs={{0,1},{1,2},{2,3},{4,5},{5,6},{6,7},{8,9},{9,10},{10,11},{12,13},{... | collective-permute-start | bytes 884744 | tf_op jit(solution)/shard_map/ppermute | solution.py:20
  93.9 10.7 %collective-permute-start.23 = (bf16[8,2,8,1152]{3,2,1,0:T(8,128)(2,1)S(1)}, bf16[8,2,8,1152]{3,2,1,0:T(8,128)(2,1)S(1)}, u32[]{:S(2)}, u32[]{:S(2)}) collective-permute-start(bf16[8,2,8,1152]{3,2,1,0:T(8,128)(2,1)S(1)} %get-tuple-element.180), channel_id=1, source_target_pairs={{1,0},{2,1},{3,2},{5,4},{6,5},{7,6},{9,8},{10,9},{11,10},{13,12},{... | collective-permute-start | bytes 884744 | tf_op jit(solution)/shard_map/ppermute | solution.py:20
  95.5 9.3 %collective-permute-start.13 = (bf16[16,2,8,128]{3,2,1,0:T(8,128)(2,1)S(1)}, bf16[16,2,8,128]{3,2,1,0:T(8,128)(2,1)S(1)}, u32[]{:S(2)}, u32[]{:S(2)}) collective-permute-start(bf16[16,2,8,128]{3,2,1,0:T(8,128)(2,1)S(1)} %slice.395), channel_id=1, source_target_pairs={{0,4},{4,8},{8,12},{1,5},{5,9},{9,13},{2,6},{6,10},{10,14},{3,7},{... | collective-permute-start | bytes 196616 | tf_op jit(solution)/shard_map/ppermute | solution.py:20
  (4 other events, 7.3 us)
